TPU v7x, 32 devices: a whole 2x2x4 slice. The times are simulated.
32 devices in a mesh: seq: 16 (over z, x, core), tp: 2 (over y).
Axes of the slice: x: 2, y: 2, z: 4, core: 2. Of those that a mesh axis runs over, the one named last changes fastest.
Arguments:
- tokens: bfloat16 [8192, 5376], P(('seq', 'tp')), may hold values from -6 to 6
- norm_gain: float32 [5376], replicated, may hold values from 0.5 to 1.5
- w_query: bfloat16 [5376, 2048], P(None, 'tp'), may hold values from -0.078125 to 0.078125
- key_value_weight: bfloat16 [5376, 2048], P(None, 'tp'), may hold values from -0.078125 to 0.078125
- query_gain: float32 [128], replicated, may hold values from 0.5 to 7
- key_gain: float32 [128], replicated, may hold values from 0.5 to 7
- lengths: int32 [8], replicated, may hold values from 1 to 4096, as said below
- segment_ids: int32 [8192], P('seq'), may hold values from 0 to 7, as said below
- req_counts: int32 [8], replicated, may hold values from 8 to 16, as said below
- req_slots: int32 [128], replicated, may hold values from 0 to 131071, as said below
Outputs:
- attended: bfloat16 [8192, 2048], P('seq', 'tp')
- cache: bfloat16 [131072, 2048], P('seq', 'tp')
Inputs may be any that keep to these rules, and one draw needn't show every extreme that they name: lengths sum to 8192; the longest is exactly 4096. Prompts lie in order: prompt p covers lengths[p] consecutive tokens, so segment_ids never falls. `req_counts`: the requests of prompt p follow those of prompts before it; entries past all requests are unused. `req_slots`: the cache rows of different requests never intersect and lie within the cache; unused entries are 0.
All inputs are finite; a program needn't handle non-finite values.
Results may differ from a plain program's by a relative error of at most 0.005.
The roundings to bfloat16 on the way count: a program that leaves them out, or rounds other values in their place, can miss the bound.
Values may be sent and summed in bfloat16 or wider, within the bound.
No kernel may reach another device: no remote copies, remote signals or barrier semaphores. Data moves between devices by JAX's collectives and lax.ppermute only.
A program may use at most 192 MiB of HBM per device.

v0:
```python
import math

import jax
import jax.numpy as jnp
from jax import lax
from jax.sharding import PartitionSpec as P

CACHE_DEV = 8192


rope_base = 1000000.0
query_scalar = 168.0
epsilon = 1e-06


def rms_scale(values, gains):
    return values * lax.rsqrt(jnp.mean(values * values, axis=-1, keepdims=True) + epsilon) * gains


def rope_table(positions, head_width):
    half_width = head_width // 2
    frequency = jnp.exp(
        jnp.arange(half_width, dtype=jnp.float32) * (-2.0 * math.log(rope_base) / head_width)
    )
    angles = positions.astype(jnp.float32)[:, None] * frequency[None, :]
    return (jnp.cos(angles), jnp.sin(angles))


def rotate_pairs(values, cosine, sine_table):
    half_width = values.shape[-1] // 2
    front_half = values[..., :half_width]
    back_half = values[..., half_width:]
    cos_part = cosine[:, None, :]
    sin_part = sine_table[:, None, :]
    return jnp.concatenate(
        [
            front_half * cos_part - back_half * sin_part,
            back_half * cos_part + front_half * sin_part,
        ],
        axis=-1,
    )


def project(tokens, norm_gain, w_query, key_value_weight, query_gain, key_gain, positions):
    token_count = tokens.shape[0]
    head_width = query_gain.shape[0]
    as_float = tokens.astype(jnp.float32)
    normed = rms_scale(as_float, norm_gain).astype(jnp.bfloat16)
    query_raw = jnp.dot(normed, w_query, preferred_element_type=jnp.float32)
    keyval_raw = jnp.dot(normed, key_value_weight, preferred_element_type=jnp.float32)
    cosine, sine_table = rope_table(positions, head_width)
    query_rows = rotate_pairs(
        rms_scale(query_raw.reshape(token_count, -1, head_width), query_gain), cosine, sine_table
    ) * query_scalar ** (-0.5)
    split_kv = keyval_raw.reshape(token_count, -1, 2, head_width)
    keys = rotate_pairs(rms_scale(split_kv[:, :, 0], key_gain), cosine, sine_table)
    key_value_rows = (
        jnp.stack([keys, split_kv[:, :, 1]], axis=2).reshape(token_count, -1).astype(jnp.bfloat16)
    )
    return (query_rows.reshape(token_count, -1).astype(jnp.bfloat16), key_value_rows)


def prompt_starts(segment_ids, lengths):
    starts = jnp.cumsum(lengths) - lengths
    prompt_ids = jnp.arange(lengths.shape[0], dtype=jnp.int32)
    chosen = jnp.where(segment_ids[:, None] == prompt_ids[None, :], starts[None, :], jnp.int32(0))
    return jnp.sum(chosen, axis=1)


def sources(cache_index, lengths, req_counts, req_slots):
    starts = jnp.cumsum(lengths) - lengths
    prompt_ids = jnp.arange(lengths.shape[0], dtype=jnp.int32)
    request_ids = jnp.arange(req_slots.shape[0], dtype=jnp.int32)
    request_ends = jnp.cumsum(req_counts)
    owner_prompt = jnp.sum(
        (request_ends[None, :] <= request_ids[:, None]).astype(jnp.int32), axis=1
    )
    matches = owner_prompt[:, None] == prompt_ids[None, :]
    request_length = jnp.sum(jnp.where(matches, lengths[None, :], jnp.int32(0)), axis=1)
    request_start = jnp.sum(jnp.where(matches, starts[None, :], jnp.int32(0)), axis=1)
    inside = (cache_index[:, None] >= req_slots[None, :]) & (
        cache_index[:, None] < req_slots[None, :] + request_length[None, :]
    )
    offsets = request_start[None, :] + cache_index[:, None] - req_slots[None, :]
    source_row = jnp.sum(jnp.where(inside, offsets, jnp.int32(0)), axis=1)
    source_live = jnp.max(inside.astype(jnp.int32), axis=1) > 0
    return (source_row, source_live)


def on_device(
    tokens,
    norm_gain,
    w_query,
    key_value_weight,
    query_gain,
    key_gain,
    lengths,
    segment_ids,
    req_counts,
    req_slots,
):
    gathered = lax.all_gather(tokens, "tp", axis=0, tiled=True)
    row_count = gathered.shape[0]
    seq_rank = lax.axis_index("seq")
    first_row = seq_rank * row_count
    query_index = first_row + jnp.arange(row_count, dtype=jnp.int32)
    positions = query_index - prompt_starts(segment_ids, lengths)
    query_rows, key_value_rows = project(
        gathered, norm_gain, w_query, key_value_weight, query_gain, key_gain, positions
    )
    head_width = query_gain.shape[0]
    kv_heads = key_value_rows.shape[1] // (2 * head_width)
    query_heads = query_rows.reshape(row_count, kv_heads, 2, head_width)
    cache_index = seq_rank * CACHE_DEV + jnp.arange(CACHE_DEV, dtype=jnp.int32)
    source_row, source_live = sources(cache_index, lengths, req_counts, req_slots)

    def attend_block(state_now, key_block, seg_block, block_start):
        maxima, totals, running = state_now
        key_count = key_block.shape[0]
        grouped_heads = key_block.reshape(key_count, kv_heads, 2, head_width)
        key_part = grouped_heads[:, :, 0]
        value_part = grouped_heads[:, :, 1]
        key_index = block_start + jnp.arange(key_count, dtype=jnp.int32)
        allowed = (seg_block[None, :] == segment_ids[:, None]) & (
            key_index[None, :] <= query_index[:, None]
        )
        scores = jnp.einsum(
            "qgrd,kgd->grqk", query_heads, key_part, preferred_element_type=jnp.float32
        )
        new_maxima = jnp.maximum(maxima, jnp.max(jnp.where(allowed, scores, -1e30), axis=-1))
        factor = jnp.exp(maxima - new_maxima)
        exp_scores = jnp.where(allowed, jnp.exp(scores - new_maxima[..., None]), 0.0)
        totals = totals * factor + jnp.sum(exp_scores, axis=-1)
        weighted = jnp.einsum(
            "grqk,kgd->qgrd",
            exp_scores.astype(jnp.bfloat16),
            value_part,
            preferred_element_type=jnp.float32,
        )
        running = running * jnp.transpose(factor, (2, 0, 1))[..., None] + weighted
        return (new_maxima, totals, running)

    def attend_piece(state_now, key_block, seg_block, block_start):
        return attend_block(state_now, key_block, seg_block, block_start)

    initial = (
        jnp.full((kv_heads, 2, row_count), -1e30, jnp.float32),
        jnp.zeros((kv_heads, 2, row_count), jnp.float32),
        jnp.zeros((row_count, kv_heads, 2, head_width), jnp.float32),
    )
    key_block = lax.all_gather(key_value_rows, "seq", axis=0, tiled=True)
    seg_block = lax.all_gather(segment_ids, "seq", axis=0, tiled=True)
    key_count = key_block.shape[0]
    block_span = 512

    def inner(counter, current):
        offset = counter * block_span
        key_slice = lax.dynamic_slice_in_dim(key_block, offset, block_span, 0)
        seg_slice = lax.dynamic_slice_in_dim(seg_block, offset, block_span, 0)
        return attend_piece(current, key_slice, seg_slice, offset)

    final_state = lax.fori_loop(0, key_count // block_span, inner, initial)
    every_row = lax.all_gather(key_value_rows, "seq", axis=0, tiled=True)
    picked = jnp.take(every_row, source_row, axis=0)
    cache = jnp.where(source_live[:, None], picked, jnp.zeros_like(picked))
    maxima, totals, running = final_state
    attended = (
        (running / jnp.transpose(totals, (2, 0, 1))[..., None])
        .reshape(row_count, -1)
        .astype(jnp.bfloat16)
    )
    return (attended, cache)


def solution(mesh):
    placed = (
        P(("seq", "tp"), None),
        P(),
        P(None, "tp"),
        P(None, "tp"),
        P(),
        P(),
        P(),
        P("seq"),
        P(),
        P(),
    )
    return jax.shard_map(
        on_device,
        mesh=mesh,
        in_specs=placed,
        out_specs=(P("seq", "tp"), P("seq", "tp")),
        check_vma=False,
    )
```

profile of v0, /device:TPU:31, one launch (start us, length us, event | category | flops | bytes accessed | tf_op | source)
XLA Modules:
  0.0 473.2 jit_solution(2000407036407505934)
XLA Ops:
  11.2 69.9 %all-gather.4.cloned.1.call-done = bf16[512,5376]{1,0:T(8,128)(2,1)} async-done(((bf16[256,5376]{1,0:T(8,128)(2,1)}), bf16[512,5376]{1,0:T(8,128)(2,1)}) %all-gather.4.cloned.1.call-update) | async-done | bytes 5505040 | tf_op jit(solution)/shard_map/all_gather | solution.py:102
  81.1 3.9 fusion.19
  85.3 8.7 %fusion.24 = f32[512,1024]{1,0:T(8,128)S(1)} fusion(bf16[5376,1024]{1,0:T(8,128)(2,1)} %param.15, bf16[512,5376]{1,0:T(8,128)(2,1)S(1)} %copy-done.1, f32[5376]{0:T(1024)S(1)} %copy-done.7, f32[512]{0:T(512)S(1)} %add_rsqrt_fusion.2), kind=kOutput, calls=%fused_computation.46 | convolution fusion | flops 5648154624 | bytes 18635776 | tf_op jit(solution)/shard_map/dot_general | solution.py:50
  94.0 2.8 reshape.208
  96.7 2.3 slice.45
  99.1 2.7 slice.48
  106.5 17.4 %all-gather = s32[16,1,512]{2,1,0:T(1,128)S(1)} all-gather(s32[1,1,512]{2,1,0:T(1,128)S(1)} %bitcast.91), channel_id=1, replica_groups=mesh['seq'=16,'tp'=2] {'seq'}, dimensions={0}, use_global_device_ids=true | all-gather | bytes 34816 | tf_op jit(solution)/shard_map/all_gather | solution.py:152
  124.0 3.7 convert_reduce_fusion
  127.7 10.4 %convolution_bitcast_fusion = f32[64,8,8,128]{3,1,2,0:T(8,128)S(1)} fusion(bf16[5376,1024]{1,0:T(8,128)(2,1)} %param.14, bf16[512,5376]{1,0:T(8,128)(2,1)} %all-gather.4.cloned.1.call-done, f32[5376]{0:T(1024)S(1)} %copy-done.7, f32[512]{0:T(512)S(1)} %add_rsqrt_fusion.2), kind=kOutput, calls=%fused_computation.45 | convolution fusion | flops 5648154624 | bytes 18635776 | tf_op jit(solution)/shard_map/dot_general | solution.py:49
  145.6 86.3 %all-gather.6.cloned.1.call-done = bf16[8192,1024]{1,0:T(8,128)(2,1)} async-done(((bf16[512,1024]{1,0:T(8,128)(2,1)}), bf16[8192,1024]{1,0:T(8,128)(2,1)}) %all-gather.6.cloned.1.call-update) | async-done | bytes 16777232 | tf_op jit(solution)/shard_map/all_gather | solution.py:151
  231.9 169.9 %while.18 = (s32[]{:T(128)}, f32[4,2,512]{2,1,0:T(2,128)S(1)}, f32[4,2,512]{2,1,0:T(2,128)S(1)}, f32[512,4,2,128]{0,3,2,1:T(8,128)S(1)}, s32[8192]{0:T(1024)S(1)...) while((s32[]{:T(128)}, f32[4,2,512]{2,1,0:T(2,128)S(1)}, ...), condition=%wide.region_8.9_spmd.clone, body=%wide.region_5.8_spmd.clone.sunk | while | flops 1092903936 | bytes 36978892 | solution.py:162
  232.3 2.3 constant_dynamic-slice_fusion.2
  236.1 2.7 fusion.38
  242.9 2.3 constant_dynamic-slice_fusion.2
  246.7 2.7 fusion.38
  250.9 2.2 bitcast_add_fusion.2
  253.5 2.3 constant_dynamic-slice_fusion.2
  257.3 2.7 fusion.38
  261.5 2.2 bitcast_add_fusion.2
  264.2 2.3 constant_dynamic-slice_fusion.2
  267.9 2.7 fusion.38
  272.1 2.2 bitcast_add_fusion.2
  274.8 2.3 constant_dynamic-slice_fusion.2
  278.5 2.7 fusion.38
  285.4 2.3 constant_dynamic-slice_fusion.2
  289.2 2.7 fusion.38
  296.0 2.3 constant_dynamic-slice_fusion.2
  299.8 2.7 fusion.38
  306.6 2.3 constant_dynamic-slice_fusion.2
  310.4 2.7 fusion.38
  317.2 2.3 constant_dynamic-slice_fusion.2
  321.0 2.7 fusion.38
  327.9 2.3 constant_dynamic-slice_fusion.2
  331.6 2.7 fusion.38
  338.5 2.3 constant_dynamic-slice_fusion.2
  342.3 2.7 fusion.38
  349.1 2.3 constant_dynamic-slice_fusion.2
  352.9 2.7 fusion.38
  359.7 2.3 constant_dynamic-slice_fusion.2
  363.5 2.7 fusion.38
  370.3 2.3 constant_dynamic-slice_fusion.2
  374.1 2.7 fusion.38
  381.0 2.3 constant_dynamic-slice_fusion.2
  384.7 2.7 fusion.38
  391.6 2.3 constant_dynamic-slice_fusion.2
  395.3 2.7 fusion.38
  403.4 48.4 %gather_fusion = bf16[8192,1024]{1,0:T(8,128)(2,1)} fusion(bf16[8192,1024]{1,0:T(8,128)(2,1)} %get-tuple-element.382, s32[8192]{0:T(1024)S(1)} %broadcast_clamp_fusion), kind=kCustom, calls=%fused_computation | custom fusion | bytes 33587200 | tf_op jit(solution)/shard_map/jit(_take)/gather | solution.py:164
  451.8 14.6 %select_select_fusion = bf16[8192,1024]{1,0:T(8,128)(2,1)} fusion(bf16[8192,1024]{1,0:T(8,128)(2,1)} %gather_fusion, pred[8192]{0:T(1024)(128)(4,1)S(1)} %get-tuple-element.271, pred[8192]{0:T(1024)(128)(4,1)S(1)} %get-tuple-element.272), kind=kLoop, calls=%fused_computation.29 | loop fusion | flops 16777216 | bytes 33570816 | tf_op jit(solution)/shard_map/jit(_where)/select_n | solution.py:165
  (201 shorter events, 101.1 us)
Async XLA Ops:
  7.2 77.8 %copy-start.7 = (f32[5376]{0:T(1024)S(1)}, f32[5376]{0:T(1024)}, u32[]{:S(2)}) copy-start(f32[5376]{0:T(1024)} %param.13) | copy-start | bytes 64516
  7.2 73.9 %all-gather.4.cloned.1.call-start = ((), (), s32[]{:S(2)}) async-start(), calls=%async_computation | async-start | bytes 8257536 | tf_op jit(solution)/shard_map/all_gather | solution.py:102
  7.9 224.0 %all-gather.6.cloned.1.call-start = ((), (), s32[]{:S(2)}) async-start(), calls=%async_computation.1 | async-start | bytes 17825792 | tf_op jit(solution)/shard_map/all_gather | solution.py:151
  81.1 4.2 copy-start.1
  96.7 5.5 %copy-start.3 = (f32[128]{0:T(128)S(1)}, f32[128]{0:T(128)}, u32[]{:S(2)}) copy-start(f32[128]{0:T(128)} %param.17) | copy-start | bytes 1540
  103.0 3.2 copy-start.8
  103.0 3.4 copy-start.6
  103.0 3.5 copy-start.4
  103.0 3.5 copy-start.2
  138.1 2.7 copy-start.5
  138.6 1.3 copy-start
Sparse Core Ops, SparseCore 0:
  9.5 71.4 all-gather.3
  106.2 125.6 all-gather.5
where the time goes:
time: 479 us; the launch traced here: 473 us
  waiting for transfers between devices  157 us (33%)
  local copies, waits for them, and re-layouts  125 us (26%)
  matrix products  97.2 us (20%)
  other arithmetic  61 us (13%)
  blocking collectives  17.4 us (4%)
  between operations  14.4 us (3%)
    all_gather x1, waiting for transfers between devices, on_device(): key_block = lax.all_gather(key_value_rows, 'seq', axis=0, tiled=True)  86.3 us
    all_gather x1, waiting for transfers between devices, on_device(): gathered = lax.all_gather(tokens, 'tp', axis=0, tiled=True)  69.9 us
    dynamic_slice x32, local copies, waits for them, and re-layouts, inner(): key_slice = lax.dynamic_slice_in_dim(key_block, offset, block_span, 0)  60.2 us
    gather x1, local copies, waits for them, and re-layouts, on_device(): picked = jnp.take(every_row, source_row, axis=0)  48.4 us
    dot_general x16, matrix products, attend_block(): jnp.einsum('qgrd,kgd->grqk', query_heads, key_part, preferred_element_typ...  42.8 us
    dot_general x16, matrix products, attend_block(): jnp.einsum('grqk,kgd->qgrd', exp_scores.astype(jnp.bfloat16), value_part,...  35.3 us
    reduce_sum x16, other arithmetic, attend_block(): totals = totals * factor + jnp.sum(exp_scores, axis=-1)  23.6 us
    all_gather x1, blocking collectives, on_device(): seg_block = lax.all_gather(segment_ids, 'seq', axis=0, tiled=True)  17.4 us
  transfers between devices with their start and end apart: 2, of which 2 were waited for; matrix products, arithmetic and copies ran while one was open for 5% of the time, Pallas kernels for 0%

commit v1 on v0

--- a/solution.py
+++ b/solution.py
@@ -87,6 +87,20 @@
     return (source_row, source_live)
 
 
+def gather_tp(tokens):
+    tp_size = lax.axis_size("tp")
+    tp_rank = lax.axis_index("tp")
+    rows = tokens.shape[0]
+    gathered = jnp.zeros((tp_size * rows,) + tokens.shape[1:], tokens.dtype)
+    gathered = lax.dynamic_update_slice_in_dim(gathered, tokens, tp_rank * rows, 0)
+    for shift in range(1, tp_size):
+        pairs = [(i, (i + shift) % tp_size) for i in range(tp_size)]
+        got = lax.ppermute(tokens, "tp", pairs)
+        source = (tp_rank - shift) % tp_size
+        gathered = lax.dynamic_update_slice_in_dim(gathered, got, source * rows, 0)
+    return gathered
+
+
 def on_device(
     tokens,
     norm_gain,
@@ -99,29 +113,31 @@
     req_counts,
     req_slots,
 ):
-    gathered = lax.all_gather(tokens, "tp", axis=0, tiled=True)
+    gathered = gather_tp(tokens)
     row_count = gathered.shape[0]
     seq_rank = lax.axis_index("seq")
     first_row = seq_rank * row_count
     query_index = first_row + jnp.arange(row_count, dtype=jnp.int32)
-    positions = query_index - prompt_starts(segment_ids, lengths)
+    segment_start = prompt_starts(segment_ids, lengths)
+    positions = query_index - segment_start
     query_rows, key_value_rows = project(
         gathered, norm_gain, w_query, key_value_weight, query_gain, key_gain, positions
     )
     head_width = query_gain.shape[0]
     kv_heads = key_value_rows.shape[1] // (2 * head_width)
     query_heads = query_rows.reshape(row_count, kv_heads, 2, head_width)
-    cache_index = seq_rank * CACHE_DEV + jnp.arange(CACHE_DEV, dtype=jnp.int32)
+    cache_rows = CACHE_DEV
+    cache_index = seq_rank * cache_rows + jnp.arange(cache_rows, dtype=jnp.int32)
     source_row, source_live = sources(cache_index, lengths, req_counts, req_slots)
 
-    def attend_block(state_now, key_block, seg_block, block_start):
+    def attend_block(state_now, key_block, block_start):
         maxima, totals, running = state_now
         key_count = key_block.shape[0]
         grouped_heads = key_block.reshape(key_count, kv_heads, 2, head_width)
         key_part = grouped_heads[:, :, 0]
         value_part = grouped_heads[:, :, 1]
         key_index = block_start + jnp.arange(key_count, dtype=jnp.int32)
-        allowed = (seg_block[None, :] == segment_ids[:, None]) & (
+        allowed = (key_index[None, :] >= segment_start[:, None]) & (
             key_index[None, :] <= query_index[:, None]
         )
         scores = jnp.einsum(
@@ -140,28 +156,23 @@
         running = running * jnp.transpose(factor, (2, 0, 1))[..., None] + weighted
         return (new_maxima, totals, running)
 
-    def attend_piece(state_now, key_block, seg_block, block_start):
-        return attend_block(state_now, key_block, seg_block, block_start)
-
     initial = (
         jnp.full((kv_heads, 2, row_count), -1e30, jnp.float32),
         jnp.zeros((kv_heads, 2, row_count), jnp.float32),
         jnp.zeros((row_count, kv_heads, 2, head_width), jnp.float32),
     )
+    block_span = row_count
+    state = attend_block(initial, key_value_rows, first_row)
     key_block = lax.all_gather(key_value_rows, "seq", axis=0, tiled=True)
-    seg_block = lax.all_gather(segment_ids, "seq", axis=0, tiled=True)
-    key_count = key_block.shape[0]
-    block_span = 512
+    first_block = jnp.min(segment_start) // block_span
 
     def inner(counter, current):
         offset = counter * block_span
         key_slice = lax.dynamic_slice_in_dim(key_block, offset, block_span, 0)
-        seg_slice = lax.dynamic_slice_in_dim(seg_block, offset, block_span, 0)
-        return attend_piece(current, key_slice, seg_slice, offset)
-
-    final_state = lax.fori_loop(0, key_count // block_span, inner, initial)
-    every_row = lax.all_gather(key_value_rows, "seq", axis=0, tiled=True)
-    picked = jnp.take(every_row, source_row, axis=0)
+        return attend_block(current, key_slice, offset)
+
+    final_state = lax.fori_loop(first_block, seq_rank, inner, state)
+    picked = jnp.take(key_block, source_row, axis=0)
     cache = jnp.where(source_live[:, None], picked, jnp.zeros_like(picked))
     maxima, totals, running = final_state
     attended = (

time: 479 us -> 367 us (0.77); the launches traced: 473 us -> 371 us
  matrix products: 97.2 us -> 61.1 us
  local copies, waits for them, and re-layouts: 125 us -> 93.5 us
  blocking collectives: 17.4 us -> 0 us
  other arithmetic: 61 us -> 47.4 us
  waiting for transfers between devices: 157 us -> 151 us
    all_gather x1 -> x0, waiting for transfers between devices: 69.9 us -> none  [on_device(): gathered = lax.all_gather(tokens, 'tp', axis=0, tiled=True)]
    ppermute x0 -> x1, waiting for transfers between devices: none -> 55.7 us  [gather_tp(): got = lax.ppermute(tokens, 'tp', pairs)]
    dynamic_slice x32 -> x16, local copies, waits for them, and re-layouts: 60.2 us -> 30.1 us  [inner(): key_slice = lax.dynamic_slice_in_dim(key_block, offset, block_span, 0)]
    dot_general x16 -> x9, matrix products: 42.8 us -> 22.8 us  [attend_block(): jnp.einsum('qgrd,kgd->grqk', query_heads, key_part, preferred_element_typ...]
    all_gather x1 -> x0, blocking collectives: 17.4 us -> none  [on_device(): seg_block = lax.all_gather(segment_ids, 'seq', axis=0, tiled=True)]
    dot_general x16 -> x9, matrix products: 35.3 us -> 20 us  [attend_block(): jnp.einsum('grqk,kgd->qgrd', exp_scores.astype(jnp.bfloat16), value_part,...]
    reduce_sum x16 -> x9, other arithmetic: 23.6 us -> 13.3 us  [attend_block(): totals = totals * factor + jnp.sum(exp_scores, axis=-1)]
    all_gather x1, waiting for transfers between devices: 86.3 us -> 95.4 us  [on_device(): key_block = lax.all_gather(key_value_rows, 'seq', axis=0, tiled=True)]
  transfers between devices with their start and end apart: 2 -> 2, of which waited for: 2 -> 2; matrix products, arithmetic and copies ran while one was open for 5% -> 9% of each run, Pallas kernels for 0% -> 0%
where the time goes in v1:
time: 367 us; the launch traced here: 371 us
  waiting for transfers between devices  151 us (41%)
  local copies, waits for them, and re-layouts  93.5 us (25%)
  matrix products  61.1 us (17%)
  other arithmetic  47.4 us (13%)
  between operations  17.2 us (5%)
    all_gather x1, waiting for transfers between devices, on_device(): key_block = lax.all_gather(key_value_rows, 'seq', axis=0, tiled=True)  95.4 us
    ppermute x1, waiting for transfers between devices, gather_tp(): got = lax.ppermute(tokens, 'tp', pairs)  55.7 us
    gather x1, local copies, waits for them, and re-layouts, on_device(): picked = jnp.take(key_block, source_row, axis=0)  48.4 us
    dynamic_slice x16, local copies, waits for them, and re-layouts, inner(): key_slice = lax.dynamic_slice_in_dim(key_block, offset, block_span, 0)  30.1 us
    dot_general x9, matrix products, attend_block(): jnp.einsum('qgrd,kgd->grqk', query_heads, key_part, preferred_element_typ...  22.8 us
    dot_general x9, matrix products, attend_block(): jnp.einsum('grqk,kgd->qgrd', exp_scores.astype(jnp.bfloat16), value_part,...  20 us
    select_n x1, other arithmetic, on_device(): cache = jnp.where(source_live[:, None], picked, jnp.zeros_like(picked))  14.6 us
    reduce_sum x9, other arithmetic, attend_block(): totals = totals * factor + jnp.sum(exp_scores, axis=-1)  13.3 us
  transfers between devices with their start and end apart: 2, of which 2 were waited for; matrix products, arithmetic and copies ran while one was open for 9% of the time, Pallas kernels for 0%

profile of v1, /device:TPU:31, one launch (start us, length us, event | category | flops | bytes accessed | tf_op | source)
XLA Modules:
  0.0 371.3 jit_solution(2958764780410404313)
XLA Ops:
  12.4 55.7 %collective-permute-done = bf16[256,5376]{1,0:T(8,128)(2,1)} collective-permute-done((bf16[256,5376]{1,0:T(8,128)(2,1)}, bf16[256,5376]{1,0:T(8,128)(2,1)}, u32[]{:S(2)}, u32[]{:S(2)}) %collective-permute-start) | collective-permute-done | bytes 2752544 | tf_op jit(solution)/shard_map/ppermute | solution.py:98
  68.1 2.1 constant_dynamic-update-slice_fusion
  72.7 7.3 %fusion.34 = f32[512,1024]{1,0:T(8,128)} fusion(bf16[5376,1024]{1,0:T(8,128)(2,1)S(1)} %bitcast.150, bf16[512,5376]{1,0:T(8,128)(2,1)S(1)} %constant_dynamic-update-slice_fusion, f32[5376]{0:T(1024)S(1)} %copy-done.9, f32[512]{0:T(512)S(1)} %add_rsqrt_fusion.2), kind=kOutput, calls=%fused_computation.55 | convolution fusion | flops 5648154624 | bytes 18635776 | tf_op jit(solution)/shard_map/dot_general | solution.py:50
  80.0 3.0 reshape.217
  91.7 3.7 convert_reduce_fusion
  95.8 11.0 %convolution_bitcast_fusion = f32[64,8,8,128]{3,1,2,0:T(8,128)S(1)} fusion(bf16[5376,1024]{1,0:T(8,128)(2,1)} %param.14, bf16[512,5376]{1,0:T(8,128)(2,1)} %copy-done.1, f32[5376]{0:T(1024)S(1)} %copy-done.9, f32[512]{0:T(512)S(1)} %add_rsqrt_fusion.2), kind=kOutput, calls=%fused_computation.54 | convolution fusion | flops 5648154624 | bytes 18635776 | tf_op jit(solution)/shard_map/dot_general | solution.py:49
  110.5 1.8 multiply_multiply_fusion
  112.4 1.7 multiply_subtract_fusion
  116.3 1.5 fusion.24
  117.8 1.8 bitcast_add_fusion.1
  119.5 95.4 %all-gather.2.cloned.1.call-done = bf16[8192,1024]{1,0:T(8,128)(2,1)} async-done(((bf16[512,1024]{1,0:T(8,128)(2,1)}), bf16[8192,1024]{1,0:T(8,128)(2,1)}) %all-gather.2.cloned.1.call-update) | async-done | bytes 16777232 | tf_op jit(solution)/shard_map/all_gather | solution.py:166
  214.9 84.7 %while.15 = (s32[]{:T(128)}, f32[4,2,512]{2,1,0:T(2,128)S(1)}, f32[4,2,512]{2,1,0:T(2,128)S(1)}, f32[512,4,2,128]{0,3,2,1:T(8,128)S(1)}, s32[]{:T(128)}, /*index...) while((s32[]{:T(128)}, f32[4,2,512]{2,1,0:T(2,128)S(1)}, ...), condition=%wide.region_11.12_spmd.clone, body=%wide.region_8.11_spmd.clone.sunk | while | flops 1092367360 | bytes 36972728 | solution.py:174
  215.2 2.3 constant_dynamic-slice_fusion.2
  217.5 1.5 copy.92
  219.0 2.7 fusion.51
  223.2 2.3 bitcast_add_fusion.3
  225.8 2.3 constant_dynamic-slice_fusion.2
  228.1 1.5 copy.92
  229.6 2.7 fusion.51
  232.3 1.5 fusion.53
  233.7 2.3 bitcast_add_fusion.3
  236.4 2.3 constant_dynamic-slice_fusion.2
  238.6 1.5 copy.92
  240.1 2.7 fusion.51
  244.3 2.3 bitcast_add_fusion.3
  247.0 2.3 constant_dynamic-slice_fusion.2
  249.2 1.5 copy.92
  250.7 2.7 fusion.51
  254.9 2.3 bitcast_add_fusion.3
  257.6 2.3 constant_dynamic-slice_fusion.2
  259.8 1.5 copy.92
  261.3 2.7 fusion.51
  265.5 2.3 bitcast_add_fusion.3
  268.2 2.3 constant_dynamic-slice_fusion.2
  270.4 1.5 copy.92
  271.9 2.7 fusion.51
  276.1 2.3 bitcast_add_fusion.3
  278.8 2.3 constant_dynamic-slice_fusion.2
  281.0 1.5 copy.92
  282.5 2.7 fusion.51
  286.7 2.3 bitcast_add_fusion.3
  289.3 2.3 constant_dynamic-slice_fusion.2
  291.6 1.5 copy.92
  293.1 2.7 fusion.51
  297.3 2.3 bitcast_add_fusion.3
  299.9 1.6 copy.79
  301.5 48.4 %gather_fusion = bf16[8192,1024]{1,0:T(8,128)(2,1)} fusion(bf16[8192,1024]{1,0:T(8,128)(2,1)} %get-tuple-element.263, s32[8192]{0:T(1024)S(1)} %broadcast_clamp_fusion), kind=kCustom, calls=%fused_computation | custom fusion | bytes 33587200 | tf_op jit(solution)/shard_map/jit(_take)/gather | solution.py:175
  349.9 14.6 %select_select_fusion = bf16[8192,1024]{1,0:T(8,128)(2,1)} fusion(bf16[8192,1024]{1,0:T(8,128)(2,1)} %gather_fusion, pred[8192]{0:T(1024)(128)(4,1)S(1)} %get-tuple-element.152, pred[8192]{0:T(1024)(128)(4,1)S(1)} %get-tuple-element.153), kind=kLoop, calls=%fused_computation.25 | loop fusion | flops 16777216 | bytes 33570816 | tf_op jit(solution)/shard_map/jit(_where)/select_n | solution.py:176
  (120 shorter events, 32.6 us)
Async XLA Ops:
  7.2 4.9 %copy-start.2 = (bf16[256,5376]{1,0:T(8,128)(2,1)S(1)}, bf16[256,5376]{1,0:T(8,128)(2,1)}, u32[]{:S(2)}) copy-start(bf16[256,5376]{1,0:T(8,128)(2,1)} %param.12) | copy-start | bytes 8257540
  7.2 207.7 %all-gather.2.cloned.1.call-start = ((), (), s32[]{:S(2)}) async-start(), calls=%async_computation | async-start | bytes 17825792 | tf_op jit(solution)/shard_map/all_gather | solution.py:166
  7.2 60.9 %collective-permute-start = (bf16[256,5376]{1,0:T(8,128)(2,1)}, bf16[256,5376]{1,0:T(8,128)(2,1)}, u32[]{:S(2)}, u32[]{:S(2)}) collective-permute-start(bf16[256,5376]{1,0:T(8,128)(2,1)} %param.12), channel_id=1, source_target_pairs={{0,1},{1,0},{2,3},{3,2},{4,5},{5,4},{6,7},{7,6},{8,9},{9,8},{10,11... | collective-permute-start | bytes 8257544 | tf_op jit(solution)/shard_map/ppermute | solution.py:98
  11.7 74.1 %copy-start.3 = (f32[512,64]{1,0:T(8,128)}, f32[512,64]{1,0:T(8,128)S(1)}, u32[]{:S(2)}) copy-start(f32[512,64]{1,0:T(8,128)S(1)} %get-tuple-element.145) | copy-start | bytes 393220
  11.7 74.1 %copy-start.4 = (f32[512,64]{1,0:T(8,128)}, f32[512,64]{1,0:T(8,128)S(1)}, u32[]{:S(2)}) copy-start(f32[512,64]{1,0:T(8,128)S(1)} %get-tuple-element.146) | copy-start | bytes 393220
  11.7 61.0 %slice-start = ((s8[11010048]{0:T(1024)(128)(4,1)}), s8[4194304]{0:T(1024)(128)(4,1)S(1)}, s32[]{:S(2)}) async-start(s8[11010048]{0:T(1024)(128)(4,1)} %bitcast.149), calls=%async_computation.1 | async-start | bytes 8388608
  12.1 60.6 %slice-start.1 = ((s8[11010048]{0:T(1024)(128)(4,1)}), s8[4194304]{0:T(1024)(128)(4,1)S(1)}, s32[]{:S(2)}) async-start(s8[11010048]{0:T(1024)(128)(4,1)} %bitcast.149), calls=%async_computation.2 | async-start | bytes 8388608
  12.4 60.3 %slice-start.2 = ((s8[11010048]{0:T(1024)(128)(4,1)}), s8[2621440]{0:T(1024)(128)(4,1)S(1)}, s32[]{:S(2)}) async-start(s8[11010048]{0:T(1024)(128)(4,1)} %bitcast.149), calls=%async_computation.3 | async-start | bytes 5242880
  12.4 60.3 %copy-start.9 = (f32[5376]{0:T(1024)S(1)}, f32[5376]{0:T(1024)}, u32[]{:S(2)}) copy-start(f32[5376]{0:T(1024)} %param.13) | copy-start | bytes 64516
  70.2 2.4 copy-start.1
  80.0 5.3 %copy-start.5 = (f32[128]{0:T(128)S(1)}, f32[128]{0:T(128)}, u32[]{:S(2)}) copy-start(f32[128]{0:T(128)} %param.17) | copy-start | bytes 1540
  85.7 4.8 %copy-start.10 = (s32[8]{0:T(128)S(1)}, s32[8]{0:T(128)}, u32[]{:S(2)}) copy-start(s32[8]{0:T(128)} %param.20) | copy-start | bytes 100
  85.8 5.8 %copy-start.8 = (s32[8]{0:T(128)S(1)}, s32[8]{0:T(128)}, u32[]{:S(2)}) copy-start(s32[8]{0:T(128)} %param.18) | copy-start | bytes 100
  85.8 5.9 %copy-start.6 = (s32[128]{0:T(128)S(1)}, s32[128]{0:T(128)}, u32[]{:S(2)}) copy-start(s32[128]{0:T(128)} %param.21) | copy-start | bytes 1540
  106.8 3.7 %copy-start.7 = (f32[128]{0:T(128)S(1)}, f32[128]{0:T(128)}, u32[]{:S(2)}) copy-start(f32[128]{0:T(128)} %param.16) | copy-start | bytes 1540
  114.9 1.4 copy-start
Sparse Core Ops, SparseCore 0:
  88.6 126.2 all-gather.1

commit v2 on v1

--- a/solution.py
+++ b/solution.py
@@ -87,18 +87,24 @@
     return (source_row, source_live)
 
 
-def gather_tp(tokens):
+def others_over_tp(tokens):
     tp_size = lax.axis_size("tp")
     tp_rank = lax.axis_index("tp")
     rows = tokens.shape[0]
-    gathered = jnp.zeros((tp_size * rows,) + tokens.shape[1:], tokens.dtype)
-    gathered = lax.dynamic_update_slice_in_dim(gathered, tokens, tp_rank * rows, 0)
+    others = jnp.zeros(((tp_size - 1) * rows,) + tokens.shape[1:], tokens.dtype)
     for shift in range(1, tp_size):
         pairs = [(i, (i + shift) % tp_size) for i in range(tp_size)]
         got = lax.ppermute(tokens, "tp", pairs)
         source = (tp_rank - shift) % tp_size
-        gathered = lax.dynamic_update_slice_in_dim(gathered, got, source * rows, 0)
-    return gathered
+        place = jnp.where(source < tp_rank, source, source - 1)
+        others = lax.dynamic_update_slice_in_dim(others, got, place * rows, 0)
+    return others
+
+
+def other_chunk_index(tp_rank, chunk_rows, other_rows):
+    place = jnp.arange(other_rows, dtype=jnp.int32) // chunk_rows
+    chunk = jnp.where(place < tp_rank, place, place + 1)
+    return chunk * chunk_rows + jnp.arange(other_rows, dtype=jnp.int32) % chunk_rows
 
 
 def on_device(
@@ -113,30 +119,55 @@
     req_counts,
     req_slots,
 ):
-    gathered = gather_tp(tokens)
-    row_count = gathered.shape[0]
+    tp_size = lax.axis_size("tp")
+    tp_rank = lax.axis_index("tp")
+    seq_size = lax.axis_size("seq")
     seq_rank = lax.axis_index("seq")
+    chunk_rows = tokens.shape[0]
+    row_count = chunk_rows * tp_size
+    other_rows = row_count - chunk_rows
     first_row = seq_rank * row_count
-    query_index = first_row + jnp.arange(row_count, dtype=jnp.int32)
     segment_start = prompt_starts(segment_ids, lengths)
-    positions = query_index - segment_start
-    query_rows, key_value_rows = project(
-        gathered, norm_gain, w_query, key_value_weight, query_gain, key_gain, positions
-    )
     head_width = query_gain.shape[0]
+
+    own_local = tp_rank * chunk_rows + jnp.arange(chunk_rows, dtype=jnp.int32)
+    own_start = jnp.take(segment_start, own_local)
+    own_q, own_kv = project(
+        tokens, norm_gain, w_query, key_value_weight, query_gain, key_gain,
+        first_row + own_local - own_start,
+    )
+    own_all = lax.all_gather(own_kv, "seq", axis=0, tiled=True)
+
+    other_tokens = others_over_tp(tokens)
+    other_tokens, own_all = lax.optimization_barrier((other_tokens, own_all))
+    other_local = other_chunk_index(tp_rank, chunk_rows, other_rows)
+    other_start = jnp.take(segment_start, other_local)
+    other_q, other_kv = project(
+        other_tokens, norm_gain, w_query, key_value_weight, query_gain, key_gain,
+        first_row + other_local - other_start,
+    )
+    other_all = lax.all_gather(other_kv, "seq", axis=0, tiled=True)
+
+    def to_block_order(own_part, other_part):
+        whole = jnp.zeros((row_count,) + own_part.shape[1:], own_part.dtype)
+        whole = whole.at[other_local].set(other_part, unique_indices=True)
+        return lax.dynamic_update_slice_in_dim(whole, own_part, tp_rank * chunk_rows, 0)
+
+    query_rows = to_block_order(own_q, other_q)
+    key_value_rows = to_block_order(own_kv, other_kv)
     kv_heads = key_value_rows.shape[1] // (2 * head_width)
     query_heads = query_rows.reshape(row_count, kv_heads, 2, head_width)
+    query_index = first_row + jnp.arange(row_count, dtype=jnp.int32)
     cache_rows = CACHE_DEV
     cache_index = seq_rank * cache_rows + jnp.arange(cache_rows, dtype=jnp.int32)
     source_row, source_live = sources(cache_index, lengths, req_counts, req_slots)
 
-    def attend_block(state_now, key_block, block_start):
+    def attend_block(state_now, key_block, key_index):
         maxima, totals, running = state_now
         key_count = key_block.shape[0]
         grouped_heads = key_block.reshape(key_count, kv_heads, 2, head_width)
         key_part = grouped_heads[:, :, 0]
         value_part = grouped_heads[:, :, 1]
-        key_index = block_start + jnp.arange(key_count, dtype=jnp.int32)
         allowed = (key_index[None, :] >= segment_start[:, None]) & (
             key_index[None, :] <= query_index[:, None]
         )
@@ -161,18 +192,35 @@
         jnp.zeros((kv_heads, 2, row_count), jnp.float32),
         jnp.zeros((row_count, kv_heads, 2, head_width), jnp.float32),
     )
-    block_span = row_count
-    state = attend_block(initial, key_value_rows, first_row)
-    key_block = lax.all_gather(key_value_rows, "seq", axis=0, tiled=True)
-    first_block = jnp.min(segment_start) // block_span
-
-    def inner(counter, current):
-        offset = counter * block_span
-        key_slice = lax.dynamic_slice_in_dim(key_block, offset, block_span, 0)
-        return attend_block(current, key_slice, offset)
-
-    final_state = lax.fori_loop(first_block, seq_rank, inner, state)
-    picked = jnp.take(key_block, source_row, axis=0)
+    first_block = jnp.min(segment_start) // row_count
+    own_key = tp_rank * chunk_rows + jnp.arange(chunk_rows, dtype=jnp.int32)
+
+    def own_step(block, current):
+        keys = lax.dynamic_slice_in_dim(own_all, block * chunk_rows, chunk_rows, 0)
+        return attend_block(current, keys, block * row_count + own_key)
+
+    def other_step(block, current):
+        keys = lax.dynamic_slice_in_dim(other_all, block * other_rows, other_rows, 0)
+        return attend_block(current, keys, block * row_count + other_local)
+
+    state = lax.fori_loop(first_block, seq_rank, own_step, initial)
+    state = attend_block(state, key_value_rows, query_index)
+    final_state = lax.fori_loop(first_block, seq_rank, other_step, state)
+
+    source_block = source_row // row_count
+    source_within = source_row % row_count
+    source_chunk = source_within // chunk_rows
+    source_place = jnp.where(source_chunk < tp_rank, source_chunk, source_chunk - 1)
+    table_row = jnp.where(
+        source_chunk == tp_rank,
+        source_block * chunk_rows + source_within % chunk_rows,
+        seq_size * chunk_rows
+        + source_block * other_rows
+        + source_place * chunk_rows
+        + source_within % chunk_rows,
+    )
+    table = jnp.concatenate([own_all, other_all], axis=0)
+    picked = jnp.take(table, table_row, axis=0)
     cache = jnp.where(source_live[:, None], picked, jnp.zeros_like(picked))
     maxima, totals, running = final_state
     attended = (

time: 367 us -> 421 us (1.15)
  the two profiles are of different devices: /device:TPU:31 before, /device:TPU:26 now
where the time goes in v2:
time: 421 us
  local copies, waits for them, and re-layouts  148 us (35%)
  other arithmetic  106 us (25%)
  matrix products  91.4 us (22%)
  waiting for transfers between devices  55.3 us (13%)
  between operations  17.7 us (4%)
    gather x1, local copies, waits for them, and re-layouts, on_device(): picked = jnp.take(table, table_row, axis=0)  48.6 us
    ppermute x1, waiting for transfers between devices, others_over_tp(): got = lax.ppermute(tokens, 'tp', pairs)  43.6 us
    dot_general x17, matrix products, attend_block(): jnp.einsum('qgrd,kgd->grqk', query_heads, key_part, preferred_element_typ...  35.5 us
    dynamic_slice x16, local copies, waits for them, and re-layouts, own_step(): keys = lax.dynamic_slice_in_dim(own_all, block * chunk_rows, chunk_rows, 0)  31.5 us
    dynamic_slice x16, local copies, waits for them, and re-layouts, other_step(): lax.dynamic_slice_in_dim(other_all, block * other_rows, other_rows, 0)  31.3 us
    dot_general x17, matrix products, attend_block(): jnp.einsum('grqk,kgd->qgrd', exp_scores.astype(jnp.bfloat16), value_part,...  26 us
    add x17, other arithmetic, attend_block(): totals = totals * factor + jnp.sum(exp_scores, axis=-1)  22.9 us
    reduce_sum x17, other arithmetic, attend_block(): totals = totals * factor + jnp.sum(exp_scores, axis=-1)  17.2 us
  transfers between devices with their start and end apart: 3, of which 2 were waited for; matrix products, arithmetic and copies ran while one was open for 33% of the time, Pallas kernels for 0%

profile of v2, /device:TPU:26, one launch (start us, length us, event | category | flops | bytes accessed | tf_op | source)
XLA Modules:
  0.0 420.9 jit_solution(6346642679679327412)
XLA Ops:
  7.2 2.4 fusion.48
  9.6 6.7 %fusion.67 = f32[256,1024]{1,0:T(8,128)S(1)} fusion(bf16[5376,1024]{1,0:T(8,128)(2,1)} %param.19, bf16[256,5376]{1,0:T(8,128)(2,1)} %param.16, f32[5376]{0:T(1024)} %param.17, f32[256]{0:T(256)S(1)} %add_rsqrt_fusion.5), kind=kOutput, calls=%fused_computation.109 | convolution fusion | flops 2824077312 | bytes 14833664 | tf_op jit(solution)/shard_map/dot_general | solution.py:50
  18.6 1.9 gather_fusion.2
  20.5 1.9 gather_fusion.1
  31.6 7.2 %convolution_bitcast_fusion = f32[32,8,8,128]{3,1,2,0:T(8,128)S(1)} fusion(bf16[5376,1024]{1,0:T(8,128)(2,1)} %param.18, bf16[256,5376]{1,0:T(8,128)(2,1)} %param.16, f32[5376]{0:T(1024)S(1)} %copy-done.22, f32[256]{0:T(256)S(1)} %add_rsqrt_fusion.5), kind=kOutput, calls=%fused_computation.93 | convolution fusion | flops 2824077312 | bytes 14833664 | tf_op jit(solution)/shard_map/dot_general | solution.py:49
  41.0 3.7 convert_reduce_fusion
  44.7 43.6 %collective-permute-done = bf16[256,5376]{1,0:T(8,128)(2,1)} collective-permute-done((bf16[256,5376]{1,0:T(8,128)(2,1)}, bf16[256,5376]{1,0:T(8,128)(2,1)}, u32[]{:S(2)}, u32[]{:S(2)}) %collective-permute-start) | collective-permute-done | bytes 2752544 | tf_op jit(solution)/shard_map/ppermute | solution.py:97
  88.3 11.6 %all-gather.3.cloned.1.call-done = bf16[4096,1024]{1,0:T(8,128)(2,1)} async-done(((bf16[256,1024]{1,0:T(8,128)(2,1)}), bf16[4096,1024]{1,0:T(8,128)(2,1)}) %all-gather.3.cloned.1.call-update) | async-done | bytes 8388624 | tf_op jit(solution)/shard_map/all_gather | solution.py:139
  99.9 2.4 fusion.51
  102.3 9.0 %fusion.63 = f32[256,1024]{1,0:T(8,128)} fusion(bf16[5376,1024]{1,0:T(8,128)(2,1)} %param.19, bf16[256,5376]{1,0:T(8,128)(2,1)} %collective-permute-done, f32[256]{0:T(256)S(1)} %add_rsqrt_fusion.4, f32[5376]{0:T(1024)S(1)} %copy-done.22), kind=kOutput, calls=%fused_computation.108 | convolution fusion | flops 2824077312 | bytes 14833664 | tf_op jit(solution)/shard_map/dot_general | solution.py:50
  111.3 2.1 reshape.545
  119.2 7.0 %convolution_bitcast_fusion.1 = f32[32,8,8,128]{3,1,2,0:T(8,128)S(1)} fusion(bf16[5376,1024]{1,0:T(8,128)(2,1)} %param.18, bf16[256,5376]{1,0:T(8,128)(2,1)} %collective-permute-done, f32[256]{0:T(256)} %copy-done.18, f32[5376]{0:T(1024)} %param.17), kind=kOutput, calls=%fused_computation.94 | convolution fusion | flops 2824077312 | bytes 14833664 | tf_op jit(solution)/shard_map/dot_general | solution.py:49
  127.6 3.1 scatter_custom_fusion.1
  134.1 2.8 scatter_custom_fusion
  142.5 5.4 %fusion.43 = (f32[4,2,512]{2,1,0:T(2,128)}, f32[4,512,512,2]{2,1,3,0:T(8,128)}) fusion(pred[512,512]{0,1:T(8,128)(4,1)S(1)} %compare_and_fusion.3, bf16[512,4,2,128]{0,3,2,1:T(8,128)(2,1)S(1)} %bitcast.245, bf16[512,4,2,128]{0,3,2,1:T(8,128)(2,1)S(1)} %bitcast.246), kind=kOutput, calls=%fused_computation.69 | convolution fusion | flops 541061120 | bytes 10240000 | tf_op jit(solution)/shard_map/qgrd,kgd->grqk/dot_general | solution.py:174
  148.8 87.2 %while.30 = (s32[]{:T(128)}, f32[4,2,512]{2,1,0:T(2,128)S(1)}, f32[4,2,512]{2,1,0:T(2,128)}, f32[512,4,2,128]{0,3,2,1:T(8,128)S(1)}, s32[]{:T(128)}, /*index=5*/...) while((s32[]{:T(128)}, f32[4,2,512]{2,1,0:T(2,128)S(1)}, ...), condition=%wide.region_12.14_spmd.clone, body=%wide.region_9.13_spmd.clone.sunk | while | flops 546714624 | bytes 23404824 | solution.py:206
  151.4 2.2 copy.193
  153.6 1.9 fusion.119
  162.5 2.0 copy.193
  173.3 2.0 copy.193
  175.3 1.9 fusion.119
  184.2 2.0 copy.193
  195.0 2.0 copy.193
  197.0 1.9 fusion.119
  205.9 2.0 copy.193
  216.7 2.0 copy.193
  218.8 1.9 fusion.119
  227.6 2.0 copy.193
  237.5 5.0 %fusion.47 = f32[4,2,512]{2,1,0:T(2,128)S(1)} fusion(f32[4,512,512,2]{2,1,3,0:T(8,128)} %get-tuple-element.344, f32[4,2,512]{2,1,0:T(2,128)S(1)} %get-tuple-element.535, pred[512,512]{0,1:T(8,128)(4,1)S(1)} %compare_and_fusion.3), kind=kLoop, calls=%fused_computation.73 | loop fusion | flops 6287360 | bytes 8683520 | tf_op jit(solution)/shard_map/reduce_sum | solution.py:180
  243.8 3.7 bitcast_add_fusion.2
  247.6 86.9 %while.31 = (s32[]{:T(128)}, f32[4,2,512]{2,1,0:T(2,128)S(1)}, f32[4,2,512]{2,1,0:T(2,128)}, f32[512,4,2,128]{0,3,2,1:T(8,128)S(1)}, s32[]{:T(128)}, /*index=5*/...) while((s32[]{:T(128)}, f32[4,2,512]{2,1,0:T(2,128)S(1)}, ...), condition=%wide.region_20.22_spmd.clone, body=%wide.region_17.21_spmd.clone.sunk | while | flops 546718720 | bytes 23404824 | solution.py:208
  250.3 2.0 copy.194
  252.3 1.9 fusion.125
  261.1 2.0 copy.194
  263.2 1.9 fusion.125
  272.0 2.0 copy.194
  274.0 1.9 fusion.125
  282.8 2.0 copy.194
  284.9 1.9 fusion.125
  293.7 2.0 copy.194
  304.5 2.0 copy.194
  306.6 1.9 fusion.125
  315.4 2.0 copy.194
  317.4 1.9 fusion.125
  326.3 2.0 copy.194
  336.8 13.7 %pad_maximum_fusion = bf16[8192,1024]{1,0:T(8,128)(2,1)} fusion(bf16[4096,1024]{1,0:T(8,128)(2,1)} %get-tuple-element.586, bf16[4096,1024]{1,0:T(8,128)(2,1)} %get-tuple-element.584), kind=kLoop, calls=%fused_computation.65 | loop fusion | flops 33554432 | bytes 33554432 | tf_op jit(solution)/shard_map/concatenate | solution.py:222
  350.5 48.6 %gather_fusion = bf16[8192,1024]{1,0:T(8,128)(2,1)} fusion(bf16[8192,1024]{1,0:T(8,128)(2,1)} %pad_maximum_fusion, s32[8192]{0:T(1024)S(1)} %copy-done.14), kind=kCustom, calls=%fused_computation.2 | custom fusion | bytes 33587200 | tf_op jit(solution)/shard_map/jit(_take)/gather | solution.py:223
  399.1 14.5 %select_select_fusion = bf16[8192,1024]{1,0:T(8,128)(2,1)} fusion(bf16[8192,1024]{1,0:T(8,128)(2,1)} %gather_fusion, pred[8192]{0:T(1024)(128)(4,1)S(1)} %get-tuple-element.347, pred[8192]{0:T(1024)(128)(4,1)S(1)} %copy-done.15), kind=kLoop, calls=%fused_computation.66 | loop fusion | flops 16777216 | bytes 33570816 | tf_op jit(solution)/shard_map/jit(_where)/select_n | solution.py:224
  (334 shorter events, 154.2 us)
Async XLA Ops:
  7.2 92.7 %all-gather.3.cloned.1.call-start = ((), (), s32[]{:S(2)}) async-start(), calls=%async_computation | async-start | bytes 8912896 | tf_op jit(solution)/shard_map/all_gather | solution.py:139
  16.4 1.9 copy-start.21
  16.4 2.1 copy-start.17
  16.4 6.4 %copy-start.16 = (f32[128]{0:T(128)S(1)}, f32[128]{0:T(128)}, u32[]{:S(2)}) copy-start(f32[128]{0:T(128)} %param.21) | copy-start | bytes 1540
  22.5 8.1 %copy-start.23 = (s32[8]{0:T(128)S(1)}, s32[8]{0:T(128)}, u32[]{:S(2)}) copy-start(s32[8]{0:T(128)} %param.24) | copy-start | bytes 100
  22.6 9.0 %copy-start.22 = (f32[5376]{0:T(1024)S(1)}, f32[5376]{0:T(1024)}, u32[]{:S(2)}) copy-start(f32[5376]{0:T(1024)} %param.17) | copy-start | bytes 64516
  24.0 0.6 copy-start.11
  24.0 90.8 %copy-start.12 = (f32[256,64]{1,0:T(8,128)}, f32[256,64]{1,0:T(8,128)S(1)}, u32[]{:S(2)}) copy-start(f32[256,64]{1,0:T(8,128)S(1)} %get-tuple-element.335) | copy-start | bytes 196612
  24.0 90.8 %copy-start.13 = (f32[256,64]{1,0:T(8,128)}, f32[256,64]{1,0:T(8,128)S(1)}, u32[]{:S(2)}) copy-start(f32[256,64]{1,0:T(8,128)S(1)} %get-tuple-element.336) | copy-start | bytes 196612
  26.5 221.1 %all-gather.5.cloned.1.call-start = ((), (), s32[]{:S(2)}) async-start(), calls=%async_computation.1 | async-start | bytes 8912896 | tf_op jit(solution)/shard_map/all_gather | solution.py:149
  26.5 61.8 %collective-permute-start = (bf16[256,5376]{1,0:T(8,128)(2,1)}, bf16[256,5376]{1,0:T(8,128)(2,1)}, u32[]{:S(2)}, u32[]{:S(2)}) collective-permute-start(bf16[256,5376]{1,0:T(8,128)(2,1)} %param.16), channel_id=1, source_target_pairs={{0,1},{1,0},{2,3},{3,2},{4,5},{5,4},{6,7},{7,6},{8,9},{9,8},{10,11... | collective-permute-start | bytes 8257544 | tf_op jit(solution)/shard_map/ppermute | solution.py:97
  31.6 8.8 %copy-start.19 = (s32[128]{0:T(128)S(1)}, s32[128]{0:T(128)}, u32[]{:S(2)}) copy-start(s32[128]{0:T(128)} %param.25) | copy-start | bytes 1540
  102.3 9.0 %copy-start.18 = (f32[256]{0:T(256)}, f32[256]{0:T(256)S(1)}, u32[]{:S(2)}) copy-start(f32[256]{0:T(256)S(1)} %add_rsqrt_fusion.4) | copy-start | bytes 3076
  126.1 4.6 %copy-start.20 = (f32[128]{0:T(128)S(1)}, f32[128]{0:T(128)}, u32[]{:S(2)}) copy-start(f32[128]{0:T(128)} %param.20) | copy-start | bytes 1540
  132.3 4.6 %copy-start.5 = (bf16[256,1024]{1,0:T(8,128)(2,1)S(1)}, bf16[256,1024]{1,0:T(8,128)(2,1)}, u32[]{:S(2)}) copy-start(bf16[256,1024]{1,0:T(8,128)(2,1)} %convert_element_type.62) | copy-start | bytes 1572868
  137.8 3.4 copy-start.6
  139.3 3.1 copy-start.4
  148.8 0.6 copy-start.8
  153.6 3.4 copy-start.2
  159.8 0.6 copy-start.8
  164.5 3.4 copy-start.2
  170.7 0.6 copy-start.8
  175.3 3.4 copy-start.2
  181.5 0.6 copy-start.8
  186.2 3.4 copy-start.2
  192.4 0.6 copy-start.8
  197.0 3.4 copy-start.2
  207.9 3.4 copy-start.2
  218.7 3.4 copy-start.2
  224.9 0.6 copy-start.8
  229.6 3.4 copy-start.2
  236.0 0.6 copy-start.9
  236.0 6.5 %copy-start = (f32[512,4,2,128]{0,3,2,1:T(8,128)}, f32[512,4,2,128]{0,3,2,1:T(8,128)S(1)}, u32[]{:S(2)}) copy-start(f32[512,4,2,128]{0,3,2,1:T(8,128)S(1)} %get-tuple-element.118) | copy-start | bytes 6291460
  237.4 5.1 %copy-start.10 = (f32[4,2,512]{2,1,0:T(2,128)S(1)}, f32[4,2,512]{2,1,0:T(2,128)}, u32[]{:S(2)}) copy-start(f32[4,2,512]{2,1,0:T(2,128)} %copy-done.9) | copy-start | bytes 49156
  237.4 6.4 %copy-start.1 = (f32[4,512,512,2]{2,1,3,0:T(8,128)S(1)}, f32[4,512,512,2]{2,1,3,0:T(8,128)}, u32[]{:S(2)}) copy-start(f32[4,512,512,2]{2,1,3,0:T(8,128)} %get-tuple-element.344) | copy-start | bytes 25165828
  247.6 0.6 copy-start.7
  252.3 3.4 copy-start.3
  263.2 3.4 copy-start.3
  274.0 3.4 copy-start.3
  280.2 0.6 copy-start.7
  284.9 3.4 copy-start.3
  291.0 0.6 copy-start.7
  295.7 3.4 copy-start.3
  306.6 3.4 copy-start.3
  317.4 3.4 copy-start.3
  328.3 3.4 copy-start.3
  336.8 13.7 %copy-start.14 = (s32[8192]{0:T(1024)S(1)}, s32[8192]{0:T(1024)}, u32[]{:S(2)}) copy-start(s32[8192]{0:T(1024)} %broadcast_clamp_fusion) | copy-start | bytes 98308
  350.5 48.6 %copy-start.15 = (pred[8192]{0:T(1024)(128)(4,1)S(1)}, pred[8192]{0:T(1024)(128)(4,1)}, u32[]{:S(2)}) copy-start(pred[8192]{0:T(1024)(128)(4,1)} %get-tuple-element.348) | copy-start | bytes 24580
  (7 other events, 4.2 us)
Sparse Core Ops, SparseCore 0:
  26.6 73.2 all-gather.2
  117.2 73.1 all-gather.4
